TPU v7x, 256 devices: a whole 4x4x8 slice. The times are simulated.
256 devices in a mesh: ent: 64 (over z, y, core), rep: 4 (over x).
Axes of the slice: x: 4, y: 4, z: 8, core: 2. Of those that a mesh axis runs over, the one named last changes fastest.
Arguments:
- table: float32 [262144, 256], P('ent'), may hold values from -6.1 to 6.1
- relations: float32 [824, 256], P('rep'), may hold values from -4 to 4
- anchor: int32 [2048], P('rep'), may hold values from 0 to 262143
- rel_one: int32 [2048], P('rep'), may hold values from 0 to 823
- rel_two: int32 [2048], P('rep'), may hold values from 0 to 823
Outputs:
- log_answer: float32 [2048, 262144], P('rep', 'ent')
All inputs are finite; a program needn't handle non-finite values.
Results may differ from a plain program's by a relative error of at most 0.00018.
Values sent between devices are 32-bit elements; how exact they have to be, the bound alone decides.
No kernel may reach another device: no remote copies, remote signals or barrier semaphores. Data moves between devices by JAX's collectives and lax.ppermute only.
A program may use at most 128 MiB of HBM per device.

v0:
```python
import jax
import jax.numpy as jnp
from jax import lax
from jax.sharding import PartitionSpec as P


def cmul(left, right):
    half = left.shape[1] // 2
    lre, lim = (left[:, :half], left[:, half:])
    rre, rim = (right[:, :half], right[:, half:])
    return jnp.concatenate([lre * rre - lim * rim, lre * rim + lim * rre], axis=1)


def against(query, table):
    return lax.dot_general(
        query,
        table,
        (((1,), (1,)), ((), ())),
        precision=lax.Precision.HIGHEST,
        preferred_element_type=jnp.float32,
    )


def weighted(weights, table):
    return jnp.dot(
        weights, table, precision=lax.Precision.HIGHEST, preferred_element_type=jnp.float32
    )


def on_device(table, relations, anchor, rel_one, rel_two):
    rows = table.shape[0]
    start = lax.axis_index("ent") * rows
    offset = anchor - start
    inside = ((offset >= 0) & (offset < rows)).astype(jnp.float32)
    local_rows = jnp.take(table, jnp.clip(offset, 0, rows - 1), axis=0)
    anchor_emb = lax.psum(local_rows * inside[:, None], "ent")
    rel_all = lax.all_gather(relations, "rep", axis=0, tiled=True)
    rel_first = jnp.take(rel_all, rel_one, axis=0)
    rel_second = jnp.take(rel_all, rel_two, axis=0)
    query_one = cmul(anchor_emb, rel_first)
    scores = against(query_one, table)
    local_peak = jnp.max(scores, axis=1)
    peak = lax.pmax(local_peak, "ent")
    weights = jnp.exp(scores - peak[:, None])
    total, summed = lax.psum((jnp.sum(weights, axis=1), weighted(weights, table)), "ent")
    query_two = cmul(summed / total[:, None], rel_second)
    scores_two = against(query_two, table)
    local_top = jnp.max(scores_two, axis=1)
    top = lax.pmax(local_top, "ent")
    shifted = scores_two - top[:, None]
    mass = lax.psum(jnp.sum(jnp.exp(shifted), axis=1), "ent")
    return shifted - jnp.log(mass)[:, None]


def solution(mesh):
    in_specs = (P("ent", None), P("rep", None), P("rep"), P("rep"), P("rep"))
    out_specs = P("rep", "ent")
    return jax.shard_map(
        on_device, mesh=mesh, in_specs=in_specs, out_specs=out_specs, check_vma=False
    )
```

profile of v0, /device:TPU:1, one launch (start us, length us, event | category | flops | bytes accessed | tf_op | source)
XLA Modules:
  0.0 810.7 jit_solution(4289145787885844124)
XLA Ops:
  6.5 0.0 all-reduce.3.cloned.1.call-start
  6.5 0.7 compare_and_fusion.2
  7.2 3.8 gather_fusion
  11.0 1.0 select_multiply_fusion
  12.0 0.0 all-reduce.3.cloned.1.call-update
  12.0 0.0 all-reduce.5.cloned.1.call-start
  12.1 0.7 compare_and_fusion.1
  12.8 0.7 compare_select_fusion.1
  13.4 0.7 compare_and_fusion
  14.1 0.7 compare_select_fusion
  14.8 13.3 %all-gather = f32[4,206,256]{2,1,0:T(8,128)S(1)} all-gather(f32[1,206,256]{2,1,0:T(8,128)} %bitcast.4), channel_id=1, replica_groups=mesh['ent'=64,'rep'=4] {'rep'}, dimensions={0}, use_global_device_ids=true | all-gather | bytes 1054720 | tf_op jit(solution)/shard_map/all_gather | solution.py:37
  28.1 0.1 reshape.43
  28.2 1.6 gather_fusion.1
  29.8 0.1 broadcast_select_fusion.1
  30.0 1.6 gather_fusion.2
  31.5 0.1 broadcast_select_fusion
  31.7 165.3 %all-reduce.3.cloned.1.call-done = f32[512,256]{1,0:T(8,128)} async-done(((f32[512,256]{1,0:T(8,128)}), f32[512,256]{1,0:T(8,128)}) %all-reduce.3.cloned.1.call-update) | async-done | bytes 524304 | tf_op jit(solution)/shard_map/psum | solution.py:36
  197.0 1.1 multiply_subtract_fusion.1
  198.1 10.9 %fusion.13 = (f32[512]{0:T(512)S(1)}, f32[512,4096]{1,0:T(8,128)}) fusion(f32[4096,256]{1,0:T(8,128)} %param.7, f32[512,128]{1,0:T(8,128)S(1)} %get-tuple-element.11, f32[512,128]{1,0:T(8,128)S(1)} %get-tuple-element.10), kind=kOutput, calls=%fused_computation.37 | convolution fusion | flops 6444678656 | bytes 13109248 | tf_op jit(solution)/shard_map/dot_general | solution.py:15
  209.0 126.3 %pmax.14 = f32[512]{0:T(512)S(1)} all-reduce(f32[512]{0:T(512)S(1)} %get-tuple-element.13), channel_id=1, replica_groups=mesh['ent'=64,'rep'=4] {'ent'}, use_global_device_ids=true, to_apply=%region_2.4 | all-reduce | flops 512 | bytes 4096 | tf_op jit(solution)/shard_map/pmax | solution.py:43
  335.3 11.2 %fusion.1 = f32[512,256]{1,0:T(8,128)} fusion(f32[4096,256]{1,0:T(8,128)} %param.7, f32[512,4096]{1,0:T(8,128)} %get-tuple-element.14, f32[512]{0:T(512)S(1)} %pmax.14), kind=kOutput, calls=%fused_computation.7 | convolution fusion | flops 6444548096 | bytes 13109248 | tf_op jit(solution)/shard_map/dot_general | solution.py:25
  346.5 0.0 all-reduce.5.cloned.1.call-update
  346.5 4.6 fusion
  351.1 125.4 %psum.30 = f32[512]{0:T(512)S(1)} all-reduce(f32[512]{0:T(512)S(1)} %fusion), channel_id=1, replica_groups=mesh['ent'=64,'rep'=4] {'ent'}, use_global_device_ids=true, to_apply=%region_5.7 | all-reduce | flops 512 | bytes 4096 | tf_op jit(solution)/shard_map/psum | solution.py:45
  476.5 50.5 %all-reduce.5.cloned.1.call-done = f32[512,256]{1,0:T(8,128)} async-done(((f32[512,256]{1,0:T(8,128)}), f32[512,256]{1,0:T(8,128)}) %all-reduce.5.cloned.1.call-update) | async-done | bytes 524304 | tf_op jit(solution)/shard_map/psum | solution.py:45
  527.0 1.2 broadcast_divide_fusion
  528.2 0.1 multiply_subtract_fusion
  528.3 10.9 %fusion.14 = (f32[512]{0:T(512)S(1)}, f32[512,4096]{1,0:T(8,128)}) fusion(f32[4096,256]{1,0:T(8,128)} %param.7, f32[512,128]{1,0:T(8,128)S(1)} %get-tuple-element.9, f32[512,128]{1,0:T(8,128)S(1)} %get-tuple-element.8), kind=kOutput, calls=%fused_computation.38 | convolution fusion | flops 6444678656 | bytes 13109248 | tf_op jit(solution)/shard_map/dot_general | solution.py:15
  539.2 126.3 %pmax.15 = f32[512]{0:T(512)S(1)} all-reduce(f32[512]{0:T(512)S(1)} %get-tuple-element.15), channel_id=1, replica_groups=mesh['ent'=64,'rep'=4] {'ent'}, use_global_device_ids=true, to_apply=%region_7.9 | all-reduce | flops 512 | bytes 4096 | tf_op jit(solution)/shard_map/pmax | solution.py:49
  665.5 4.6 exponential_reduce_fusion
  670.1 125.2 %psum.31 = f32[512]{0:T(512)S(1)} all-reduce(f32[512]{0:T(512)S(1)} %exponential_reduce_fusion), channel_id=1, replica_groups=mesh['ent'=64,'rep'=4] {'ent'}, use_global_device_ids=true, to_apply=%region_9.11 | all-reduce | flops 512 | bytes 4096 | tf_op jit(solution)/shard_map/psum | solution.py:51
  795.3 8.6 %subtract_subtract_fusion = f32[512,4096]{1,0:T(8,128)} fusion(f32[512,4096]{1,0:T(8,128)} %get-tuple-element.16, f32[512]{0:T(512)S(1)} %log.3, f32[512]{0:T(512)S(1)} %pmax.15), kind=kLoop, calls=%fused_computation.5 | loop fusion | flops 4194304 | bytes 16781312 | tf_op jit(solution)/shard_map/sub | solution.py:52
  (4 shorter events, 0.0 us)
Async XLA Ops:
  6.5 190.5 %all-reduce.3.cloned.1.call-start = ((), (), s32[]{:S(2)}) async-start(), calls=%async_computation | async-start | bytes 1048576 | tf_op jit(solution)/shard_map/psum | solution.py:36
  12.0 515.0 %all-reduce.5.cloned.1.call-start = ((), (), s32[]{:S(2)}) async-start(), calls=%async_computation.1 | async-start | bytes 1048576 | tf_op jit(solution)/shard_map/psum | solution.py:45
Sparse Core Ops, SparseCore 0:
  12.1 184.8 all-reduce.2
  346.6 180.3 all-reduce.4
where the time goes:
time: 811 us
  blocking collectives  516 us (64%)
  waiting for transfers between devices  216 us (27%)
  matrix products  33 us (4%)
  other arithmetic  24.9 us (3%)
  between operations  13.5 us (2%)
    psum x1, waiting for transfers between devices, on_device(): anchor_emb = lax.psum(local_rows * inside[:, None], 'ent')  165 us
    pmax x1, blocking collectives, on_device(): peak = lax.pmax(local_peak, 'ent')  126 us
    pmax x1, blocking collectives, on_device(): top = lax.pmax(local_top, 'ent')  126 us
    psum x1, blocking collectives, on_device(): lax.psum((jnp.sum(weights, axis=1), weighted(weights, table)), 'ent')  125 us
    psum x1, blocking collectives, on_device(): mass = lax.psum(jnp.sum(jnp.exp(shifted), axis=1), 'ent')  125 us
    psum x1, waiting for transfers between devices, on_device(): lax.psum((jnp.sum(weights, axis=1), weighted(weights, table)), 'ent')  50.5 us
    dot_general x2, matrix products, against(): lax.dot_general(query, table, (((1,), (1,)), ((), ())), precision=lax.Pre...  21.8 us
  transfers between devices with their start and end apart: 2, of which 2 were waited for; matrix products, arithmetic and copies ran while one was open for 1% of the time, Pallas kernels for 0%

commit v1 on v0

--- a/solution.py
+++ b/solution.py
@@ -48,7 +48,9 @@
     local_top = jnp.max(scores_two, axis=1)
     top = lax.pmax(local_top, "ent")
     shifted = scores_two - top[:, None]
-    mass = lax.psum(jnp.sum(jnp.exp(shifted), axis=1), "ent")
+    part = jnp.sum(jnp.exp(shifted), axis=1)
+    terms = lax.all_gather(part, "ent", axis=0, tiled=False)
+    mass = terms.sum(axis=0)
     return shifted - jnp.log(mass)[:, None]
 
 

time: 811 us -> 735 us (0.906)
  blocking collectives: 516 us -> 439 us
    psum x1 -> x0, blocking collectives: 125 us -> none  [on_device(): mass = lax.psum(jnp.sum(jnp.exp(shifted), axis=1), 'ent')]
    all_gather x0 -> x1, blocking collectives: none -> 48.2 us  [on_device(): terms = lax.all_gather(part, 'ent', axis=0, tiled=False)]
where the time goes in v1:
time: 735 us; the launch traced here: 734 us
  blocking collectives  439 us (60%)
  waiting for transfers between devices  216 us (29%)
  matrix products  33 us (4%)
  other arithmetic  25 us (3%)
  between operations  13.5 us (2%)
    psum x1, waiting for transfers between devices, on_device(): anchor_emb = lax.psum(local_rows * inside[:, None], 'ent')  165 us
    pmax x1, blocking collectives, on_device(): peak = lax.pmax(local_peak, 'ent')  126 us
    pmax x1, blocking collectives, on_device(): top = lax.pmax(local_top, 'ent')  126 us
    psum x1, blocking collectives, on_device(): lax.psum((jnp.sum(weights, axis=1), weighted(weights, table)), 'ent')  125 us
    psum x1, waiting for transfers between devices, on_device(): lax.psum((jnp.sum(weights, axis=1), weighted(weights, table)), 'ent')  50.5 us
    all_gather x1, blocking collectives, on_device(): terms = lax.all_gather(part, 'ent', axis=0, tiled=False)  48.2 us
    dot_general x2, matrix products, against(): lax.dot_general(query, table, (((1,), (1,)), ((), ())), precision=lax.Pre...  21.8 us
  transfers between devices with their start and end apart: 2, of which 2 were waited for; matrix products, arithmetic and copies ran while one was open for 1% of the time, Pallas kernels for 0%

profile of v1, /device:TPU:1, one launch (start us, length us, event | category | flops | bytes accessed | tf_op | source)
XLA Modules:
  0.0 733.9 jit_solution(2550703486523544713)
XLA Ops:
  6.5 0.0 all-reduce.3.cloned.1.call-start
  6.5 0.7 compare_and_fusion.2
  7.2 3.8 gather_fusion
  11.0 1.0 select_multiply_fusion
  12.0 0.0 all-reduce.3.cloned.1.call-update
  12.0 0.0 all-reduce.5.cloned.1.call-start
  12.1 0.7 compare_and_fusion.1
  12.8 0.7 compare_select_fusion.1
  13.4 0.7 compare_and_fusion
  14.1 0.7 compare_select_fusion
  14.8 13.3 %all-gather.1 = f32[4,206,256]{2,1,0:T(8,128)S(1)} all-gather(f32[1,206,256]{2,1,0:T(8,128)} %bitcast.5), channel_id=1, replica_groups=mesh['ent'=64,'rep'=4] {'rep'}, dimensions={0}, use_global_device_ids=true | all-gather | bytes 1054720 | tf_op jit(solution)/shard_map/all_gather | solution.py:37
  28.1 0.1 reshape.46
  28.2 1.6 gather_fusion.1
  29.8 0.1 broadcast_select_fusion.1
  30.0 1.6 gather_fusion.2
  31.5 0.1 broadcast_select_fusion
  31.7 165.3 %all-reduce.3.cloned.1.call-done = f32[512,256]{1,0:T(8,128)} async-done(((f32[512,256]{1,0:T(8,128)}), f32[512,256]{1,0:T(8,128)}) %all-reduce.3.cloned.1.call-update) | async-done | bytes 524304 | tf_op jit(solution)/shard_map/psum | solution.py:36
  197.0 1.1 multiply_subtract_fusion.1
  198.1 10.9 %fusion.13 = (f32[512]{0:T(512)S(1)}, f32[512,4096]{1,0:T(8,128)}) fusion(f32[4096,256]{1,0:T(8,128)} %param.7, f32[512,128]{1,0:T(8,128)S(1)} %get-tuple-element.11, f32[512,128]{1,0:T(8,128)S(1)} %get-tuple-element.10), kind=kOutput, calls=%fused_computation.37 | convolution fusion | flops 6444678656 | bytes 13109248 | tf_op jit(solution)/shard_map/dot_general | solution.py:15
  209.0 126.3 %pmax.14 = f32[512]{0:T(512)S(1)} all-reduce(f32[512]{0:T(512)S(1)} %get-tuple-element.13), channel_id=1, replica_groups=mesh['ent'=64,'rep'=4] {'ent'}, use_global_device_ids=true, to_apply=%region_2.4 | all-reduce | flops 512 | bytes 4096 | tf_op jit(solution)/shard_map/pmax | solution.py:43
  335.3 11.2 %fusion.1 = f32[512,256]{1,0:T(8,128)} fusion(f32[4096,256]{1,0:T(8,128)} %param.7, f32[512,4096]{1,0:T(8,128)} %get-tuple-element.14, f32[512]{0:T(512)S(1)} %pmax.14), kind=kOutput, calls=%fused_computation.7 | convolution fusion | flops 6444548096 | bytes 13109248 | tf_op jit(solution)/shard_map/dot_general | solution.py:25
  346.5 0.0 all-reduce.5.cloned.1.call-update
  346.5 4.6 fusion
  351.1 125.4 %psum.23 = f32[512]{0:T(512)S(1)} all-reduce(f32[512]{0:T(512)S(1)} %fusion), channel_id=1, replica_groups=mesh['ent'=64,'rep'=4] {'ent'}, use_global_device_ids=true, to_apply=%region_5.7 | all-reduce | flops 512 | bytes 4096 | tf_op jit(solution)/shard_map/psum | solution.py:45
  476.5 50.5 %all-reduce.5.cloned.1.call-done = f32[512,256]{1,0:T(8,128)} async-done(((f32[512,256]{1,0:T(8,128)}), f32[512,256]{1,0:T(8,128)}) %all-reduce.5.cloned.1.call-update) | async-done | bytes 524304 | tf_op jit(solution)/shard_map/psum | solution.py:45
  527.0 1.2 broadcast_divide_fusion
  528.2 0.1 multiply_subtract_fusion
  528.3 10.9 %fusion.14 = (f32[512]{0:T(512)S(1)}, f32[512,4096]{1,0:T(8,128)}) fusion(f32[4096,256]{1,0:T(8,128)} %param.7, f32[512,128]{1,0:T(8,128)S(1)} %get-tuple-element.9, f32[512,128]{1,0:T(8,128)S(1)} %get-tuple-element.8), kind=kOutput, calls=%fused_computation.38 | convolution fusion | flops 6444678656 | bytes 13109248 | tf_op jit(solution)/shard_map/dot_general | solution.py:15
  539.2 126.3 %pmax.15 = f32[512]{0:T(512)S(1)} all-reduce(f32[512]{0:T(512)S(1)} %get-tuple-element.15), channel_id=1, replica_groups=mesh['ent'=64,'rep'=4] {'ent'}, use_global_device_ids=true, to_apply=%region_7.9 | all-reduce | flops 512 | bytes 4096 | tf_op jit(solution)/shard_map/pmax | solution.py:49
  665.5 4.6 exponential_reduce_fusion
  670.1 48.2 %all-gather.2 = f32[64,1,512]{2,1,0:T(1,128)S(1)} all-gather(f32[1,1,512]{2,1,0:T(1,128)S(1)} %bitcast.6), channel_id=2, replica_groups=mesh['ent'=64,'rep'=4] {'ent'}, dimensions={0}, use_global_device_ids=true | all-gather | bytes 133120 | tf_op jit(solution)/shard_map/all_gather | solution.py:52
  718.3 0.1 reduce_sum.29
  718.4 8.6 %subtract_subtract_fusion = f32[512,4096]{1,0:T(8,128)} fusion(f32[512,4096]{1,0:T(8,128)} %get-tuple-element.16, f32[512]{0:T(512)S(1)} %log.7, f32[512]{0:T(512)S(1)} %pmax.15), kind=kLoop, calls=%fused_computation.5 | loop fusion | flops 4194304 | bytes 16781312 | tf_op jit(solution)/shard_map/sub | solution.py:54
  (4 shorter events, 0.0 us)
Async XLA Ops:
  6.5 190.5 %all-reduce.3.cloned.1.call-start = ((), (), s32[]{:S(2)}) async-start(), calls=%async_computation | async-start | bytes 1048576 | tf_op jit(solution)/shard_map/psum | solution.py:36
  12.0 515.0 %all-reduce.5.cloned.1.call-start = ((), (), s32[]{:S(2)}) async-start(), calls=%async_computation.1 | async-start | bytes 1048576 | tf_op jit(solution)/shard_map/psum | solution.py:45
Sparse Core Ops, SparseCore 0:
  12.1 184.8 all-reduce.2
  346.6 180.3 all-reduce.4
